TPU v7x, 32 devices: a whole 2x2x4 slice. The times are simulated.
32 devices in a mesh: dp: 4 (over z), vocab: 8 (over y, x, core).
Axes of the slice: x: 2, y: 2, z: 4, core: 2. Of those that a mesh axis runs over, the one named last changes fastest.
Arguments:
- hidden: bfloat16 [512, 8192], P('dp', 'vocab'), may hold values from -8 to 8
- out_weight: bfloat16 [19456, 8192], P('vocab', 'dp'), may hold values from -0.397747564 to 0.397747564
- token_blocks: int32 [8, 4, 16], P('vocab'), may hold values from 0 to 18, as said below
- counts: int32 [8, 4], P('vocab'), may hold values from 4 to 16, as said below
Outputs:
- allowed_logprob: float32 [8, 4, 16, 128, 128], P('vocab', 'dp')
- expected: float32 [512, 8192], P('vocab', 'dp')
Inputs may be any that keep to these rules, and one draw needn't show every extreme that they name: token_blocks[j, b, s] names one of the 19 token blocks of shard j; the entries of one list are distinct; slots at or past counts[j, b] carry no meaning. `counts`: for every beam block, some shard allows exactly 16 slots.
All inputs are finite; a program needn't handle non-finite values.
Results may differ from a plain program's by a relative error of at most 0.0021.
Values may be sent and summed in bfloat16 or wider, within the bound.
No kernel may reach another device: no remote copies, remote signals or barrier semaphores. Data moves between devices by JAX's collectives and lax.ppermute only.
A program may use at most 128 MiB of HBM per device.

v0:
```python
import jax
import jax.numpy as jnp
from jax import lax
from jax.sharding import PartitionSpec as P

D = 8192
TB = 128
BB = 128
MOST = 16


def per_device(hidden, out_weight, token_blocks, counts):
    beams_here = hidden.shape[0]
    vocab_here, columns_here = out_weight.shape
    own_blocks = beams_here // BB
    block_lists = token_blocks[0]
    block_counts = counts[0]
    weight_blocks = out_weight.reshape(vocab_here // TB, TB, columns_here)
    first_block = lax.axis_index("dp") * own_blocks
    own_counts = lax.dynamic_slice_in_dim(block_counts, first_block, own_blocks, 0)
    beam_rows = lax.all_gather(hidden, "vocab", axis=1, tiled=True)
    beam_columns = lax.all_to_all(beam_rows, "dp", split_axis=1, concat_axis=0, tiled=True)
    column_blocks = beam_columns.reshape(-1, BB, columns_here)
    pick_part = block_lists

    def partial_one_block(pair_in):
        return jnp.einsum(
            "rd,std->srt", pair_in[0], weight_blocks[pair_in[1]], preferred_element_type=jnp.float32
        )

    logits = lax.psum_scatter(
        lax.map(partial_one_block, (column_blocks, pick_part)),
        "dp",
        scatter_dimension=0,
        tiled=True,
    )
    live = jnp.arange(MOST, dtype=jnp.int32)[None, :] < own_counts[:, None]
    live_mask = live[:, :, None, None]
    masked = jnp.where(live_mask, logits, -jnp.inf)
    local_max = jnp.max(masked, axis=(1, 3))
    beam_max = lax.pmax(local_max, "vocab")
    local_total = jnp.sum(jnp.exp(masked - beam_max[:, None, :, None]), axis=(1, 3))
    beam_total = lax.psum(local_total, "vocab")
    shifted = logits - beam_max[:, None, :, None] - jnp.log(beam_total)[:, None, :, None]
    allowed_logprob = jnp.where(live_mask, shifted, 0.0)
    probabilities = jnp.where(live_mask, jnp.exp(shifted), 0.0).astype(jnp.bfloat16)
    prob_part = lax.all_gather(probabilities, "dp", axis=0, tiled=True)
    block_count = prob_part.shape[0]
    pick_part = block_lists

    def expected_one_block(pair_in):
        return jnp.einsum(
            "srt,std->rd", pair_in[0], weight_blocks[pair_in[1]], preferred_element_type=jnp.float32
        )

    embedding_part = lax.map(expected_one_block, (prob_part, pick_part)).reshape(
        block_count * BB, columns_here
    )
    summed = lax.psum_scatter(embedding_part, "vocab", scatter_dimension=0, tiled=True)
    squares = lax.psum(jnp.sum(summed * summed, axis=1), "dp")
    expected = summed * lax.rsqrt(squares / D + 1e-06)[:, None]
    return (allowed_logprob[None], expected)


def solution(mesh):
    in_specs = (P("dp", "vocab"), P("vocab", "dp"), P("vocab", None, None), P("vocab", None))
    out_specs = (P("vocab", "dp", None, None, None), P("vocab", "dp"))
    return jax.shard_map(
        per_device, mesh=mesh, in_specs=in_specs, out_specs=out_specs, check_vma=False
    )
```

profile of v0, /device:TPU:0, one launch (start us, length us, event | category | flops | bytes accessed | tf_op | source)
XLA Modules:
  0.0 437.9 jit_solution(15092039008348145845)
XLA Ops:
  9.1 31.9 %all-gather.3.cloned.1.call-done = bf16[128,8192]{0,1:T(8,128)(2,1)} async-done(((bf16[128,1024]{0,1:T(8,128)(2,1)}), bf16[128,8192]{0,1:T(8,128)(2,1)}) %all-gather.3.cloned.1.call-update) | async-done | bytes 2097168 | tf_op jit(solution)/shard_map/all_gather | solution.py:21
  45.6 48.8 %all-to-all-done = bf16[128,4,2048]{0,2,1:T(8,128)(2,1)} async-done(((bf16[128,4,2048]{0,2,1:T(8,128)(2,1)}), bf16[128,4,2048]{0,2,1:T(8,128)(2,1)}, u32[]{:S(2)}, u32[]{:S(2)}) %all-to-all-start) | async-done | bytes 2097184 | tf_op jit(solution)/shard_map/all_to_all | solution.py:22
  94.4 63.4 %while.20 = (s32[]{:T(128)}, f32[4,16,128,128]{3,2,1,0:T(8,128)}, s32[4,16]{1,0:T(4,128)S(1)}, bf16[19,128,2048]{2,1,0:T(8,128)(2,1)}, bf16[4,128,2048]{1,2,0:T(8,128)(2,1)}, /*index=5*/s32[]{:T(128)}) while((s32[]{:T(128)}, f32[4,16,128,128]{3,2,1,0:T(8,128)}, s32[4,16]{1,0:T(4,128)S(1)}, bf16[19,128,2048]{2,1,0:T(8,128)(2,1)}, ...), condition=%wide.region_1.2_spmd, body=%wide.region_0.1_spmd.sunk | while | flops 1073742848 | bytes 30938440 | solution.py:32
  94.4 8.6 %gather_fusion = bf16[16,128,2048]{2,1,0:T(8,128)(2,1)} fusion(bf16[19,128,2048]{2,1,0:T(8,128)(2,1)} %get-tuple-element.167, s32[1024]{0:T(1024)S(1)} %pad_clamp_fusion.4), kind=kCustom, calls=%fused_computation.clone.1 | custom fusion | bytes 16777280 | tf_op jit(solution)/shard_map/while/body/eval_jaxpr/gather | solution.py:28
  103.0 5.8 %convolution_bitcast_fusion.3 = f32[1,16,128,128]{2,3,1,0:T(8,128)S(1)} fusion(bf16[16,128,2048]{2,1,0:T(8,128)(2,1)} %gather_fusion, bf16[4,128,2048]{1,2,0:T(8,128)(2,1)} %get-tuple-element.168, s32[]{:T(128)} %get-tuple-element.158), kind=kOutput, calls=%fused_computation.2.clone.1 | convolution fusion | flops 1073741824 | bytes 9961984 | tf_op jit(solution)/shard_map/while/body/eval_jaxpr/rd,std->srt/dot_general | solution.py:27
  110.4 8.6 %gather_fusion = bf16[16,128,2048]{2,1,0:T(8,128)(2,1)} fusion(bf16[19,128,2048]{2,1,0:T(8,128)(2,1)} %get-tuple-element.167, s32[1024]{0:T(1024)S(1)} %pad_clamp_fusion.4), kind=kCustom, calls=%fused_computation.clone.1 | custom fusion | bytes 16777280 | tf_op jit(solution)/shard_map/while/body/eval_jaxpr/gather | solution.py:28
  119.0 5.8 %convolution_bitcast_fusion.3 = f32[1,16,128,128]{2,3,1,0:T(8,128)S(1)} fusion(bf16[16,128,2048]{2,1,0:T(8,128)(2,1)} %gather_fusion, bf16[4,128,2048]{1,2,0:T(8,128)(2,1)} %get-tuple-element.168, s32[]{:T(128)} %get-tuple-element.158), kind=kOutput, calls=%fused_computation.2.clone.1 | convolution fusion | flops 1073741824 | bytes 9961984 | tf_op jit(solution)/shard_map/while/body/eval_jaxpr/rd,std->srt/dot_general | solution.py:27
  126.2 8.6 %gather_fusion = bf16[16,128,2048]{2,1,0:T(8,128)(2,1)} fusion(bf16[19,128,2048]{2,1,0:T(8,128)(2,1)} %get-tuple-element.167, s32[1024]{0:T(1024)S(1)} %pad_clamp_fusion.4), kind=kCustom, calls=%fused_computation.clone.1 | custom fusion | bytes 16777280 | tf_op jit(solution)/shard_map/while/body/eval_jaxpr/gather | solution.py:28
  134.8 5.8 %convolution_bitcast_fusion.3 = f32[1,16,128,128]{2,3,1,0:T(8,128)S(1)} fusion(bf16[16,128,2048]{2,1,0:T(8,128)(2,1)} %gather_fusion, bf16[4,128,2048]{1,2,0:T(8,128)(2,1)} %get-tuple-element.168, s32[]{:T(128)} %get-tuple-element.158), kind=kOutput, calls=%fused_computation.2.clone.1 | convolution fusion | flops 1073741824 | bytes 9961984 | tf_op jit(solution)/shard_map/while/body/eval_jaxpr/rd,std->srt/dot_general | solution.py:27
  142.0 8.6 %gather_fusion = bf16[16,128,2048]{2,1,0:T(8,128)(2,1)} fusion(bf16[19,128,2048]{2,1,0:T(8,128)(2,1)} %get-tuple-element.167, s32[1024]{0:T(1024)S(1)} %pad_clamp_fusion.4), kind=kCustom, calls=%fused_computation.clone.1 | custom fusion | bytes 16777280 | tf_op jit(solution)/shard_map/while/body/eval_jaxpr/gather | solution.py:28
  150.6 5.8 %convolution_bitcast_fusion.3 = f32[1,16,128,128]{2,3,1,0:T(8,128)S(1)} fusion(bf16[16,128,2048]{2,1,0:T(8,128)(2,1)} %gather_fusion, bf16[4,128,2048]{1,2,0:T(8,128)(2,1)} %get-tuple-element.168, s32[]{:T(128)} %get-tuple-element.158), kind=kOutput, calls=%fused_computation.2.clone.1 | convolution fusion | flops 1073741824 | bytes 9961984 | tf_op jit(solution)/shard_map/while/body/eval_jaxpr/rd,std->srt/dot_general | solution.py:27
  159.2 73.7 %reduce-scatter.3.cloned.1.call-done = f32[1,16,128,128]{3,2,1,0:T(8,128)} async-done(((f32[4,16,128,128]{3,2,1,0:T(8,128)}), f32[1,16,128,128]{3,2,1,0:T(8,128)}) %reduce-scatter.3.cloned.1.call-update) | async-done | bytes 1048592 | tf_op jit(solution)/shard_map/reduce_scatter | solution.py:31
  234.3 13.3 %pmax.7 = f32[128]{0:T(128)S(1)} all-reduce(f32[128]{0:T(128)S(1)} %select_reduce_fusion), channel_id=1, replica_groups=mesh['dp'=4,'vocab'=8] {'vocab'}, use_global_device_ids=true, to_apply=%region_4.5 | all-reduce | flops 128 | bytes 1024 | tf_op jit(solution)/shard_map/pmax | solution.py:41
  249.2 11.8 %psum.14 = f32[1,128]{1,0:T(1,128)S(1)} all-reduce(f32[1,128]{1,0:T(1,128)S(1)} %bitcast.69), channel_id=1, replica_groups=mesh['dp'=4,'vocab'=8] {'vocab'}, use_global_device_ids=true, to_apply=%region_6.7 | all-reduce | flops 128 | bytes 1024 | tf_op jit(solution)/shard_map/psum | solution.py:43
  263.9 44.7 %all-gather.5.cloned.1.call-done = bf16[4,16,128,128]{3,2,1,0:T(8,128)(2,1)} async-done(((bf16[1,16,128,128]{3,2,1,0:T(8,128)(2,1)}), bf16[4,16,128,128]{3,2,1,0:T(8,128)(2,1)}) %all-gather.5.cloned.1.call-update) | async-done | bytes 2097168 | tf_op jit(solution)/shard_map/all_gather | solution.py:47
  308.6 57.7 %while.21 = (s32[]{:T(128)}, f32[4,128,2048]{2,1,0:T(8,128)}, bf16[4,16,128,128]{3,2,1,0:T(8,128)(2,1)}, s32[4,16]{1,0:T(4,128)S(1)}, bf16[19,128,2048]{2,1,0:T(8,128)(2,1)}, /*index=5*/s32[]{:T(128)}) while((s32[]{:T(128)}, f32[4,128,2048]{2,1,0:T(8,128)}, bf16[4,16,128,128]{3,2,1,0:T(8,128)(2,1)}, s32[4,16]{1,0:T(4,128)S(1)}, ...), condition=%wide.region_8.9_spmd, body=%wide.region_7.8_spmd.sunk | while | flops 1073742848 | bytes 26744136 | solution.py:56
  308.7 8.6 %gather_fusion.1 = bf16[16,128,2048]{2,1,0:T(8,128)(2,1)} fusion(bf16[19,128,2048]{2,1,0:T(8,128)(2,1)} %get-tuple-element.186, s32[1024]{0:T(1024)S(1)} %pad_clamp_fusion.5), kind=kCustom, calls=%fused_computation.1.clone.1 | custom fusion | bytes 16777280 | tf_op jit(solution)/shard_map/while/body/eval_jaxpr/gather | solution.py:53
  317.3 5.9 %fusion.26 = f32[4,128,2048]{2,1,0:T(8,128)} fusion(f32[4,128,2048]{2,1,0:T(8,128)} %get-tuple-element.177, s32[]{:T(128)} %get-tuple-element.176, bf16[16,128,2048]{2,1,0:T(8,128)(2,1)} %gather_fusion.1, bf16[4,16,128,128]{3,2,1,0:T(8,128)(2,1)} %get-tuple-element.184), kind=kOutput, calls=%fused_computation.13.clone.1 | convolution fusion | flops 1073741824 | bytes 9962496 | tf_op jit(solution)/shard_map/while/body/eval_jaxpr/srt,std->rd/dot_general | solution.py:52
  323.2 8.6 %gather_fusion.1 = bf16[16,128,2048]{2,1,0:T(8,128)(2,1)} fusion(bf16[19,128,2048]{2,1,0:T(8,128)(2,1)} %get-tuple-element.186, s32[1024]{0:T(1024)S(1)} %pad_clamp_fusion.5), kind=kCustom, calls=%fused_computation.1.clone.1 | custom fusion | bytes 16777280 | tf_op jit(solution)/shard_map/while/body/eval_jaxpr/gather | solution.py:53
  337.6 8.6 %gather_fusion.1 = bf16[16,128,2048]{2,1,0:T(8,128)(2,1)} fusion(bf16[19,128,2048]{2,1,0:T(8,128)(2,1)} %get-tuple-element.186, s32[1024]{0:T(1024)S(1)} %pad_clamp_fusion.5), kind=kCustom, calls=%fused_computation.1.clone.1 | custom fusion | bytes 16777280 | tf_op jit(solution)/shard_map/while/body/eval_jaxpr/gather | solution.py:53
  346.2 5.8 %fusion.26 = f32[4,128,2048]{2,1,0:T(8,128)} fusion(f32[4,128,2048]{2,1,0:T(8,128)} %get-tuple-element.177, s32[]{:T(128)} %get-tuple-element.176, bf16[16,128,2048]{2,1,0:T(8,128)(2,1)} %gather_fusion.1, bf16[4,16,128,128]{3,2,1,0:T(8,128)(2,1)} %get-tuple-element.184), kind=kOutput, calls=%fused_computation.13.clone.1 | convolution fusion | flops 1073741824 | bytes 9962496 | tf_op jit(solution)/shard_map/while/body/eval_jaxpr/srt,std->rd/dot_general | solution.py:52
  352.0 8.6 %gather_fusion.1 = bf16[16,128,2048]{2,1,0:T(8,128)(2,1)} fusion(bf16[19,128,2048]{2,1,0:T(8,128)(2,1)} %get-tuple-element.186, s32[1024]{0:T(1024)S(1)} %pad_clamp_fusion.5), kind=kCustom, calls=%fused_computation.1.clone.1 | custom fusion | bytes 16777280 | tf_op jit(solution)/shard_map/while/body/eval_jaxpr/gather | solution.py:53
  366.4 50.1 %reduce-scatter.5.cloned.1.call-done = f32[64,2048]{1,0:T(8,128)} async-done(((f32[512,2048]{1,0:T(8,128)}), f32[64,2048]{1,0:T(8,128)}) %reduce-scatter.5.cloned.1.call-update) | async-done | bytes 524304 | tf_op jit(solution)/shard_map/reduce_scatter | solution.py:59
  417.7 11.7 %psum.15 = f32[64]{0:T(128)S(1)} all-reduce(f32[64]{0:T(128)S(1)} %multiply_reduce_fusion), channel_id=1, replica_groups=mesh['dp'=4,'vocab'=8] {'dp'}, use_global_device_ids=true, to_apply=%region_11.12 | all-reduce | flops 64 | bytes 512 | tf_op jit(solution)/shard_map/psum | solution.py:60
  (51 shorter events, 34.1 us)
Async XLA Ops:
  7.2 150.7 %copy-start = (s32[1,4]{1,0:T(1,128)S(1)}, s32[1,4]{1,0:T(1,128)}, u32[]{:S(2)}) copy-start(s32[1,4]{1,0:T(1,128)} %param.11) | copy-start | bytes 52
  7.2 87.2 %copy-start.1 = (s32[1,4,16]{2,1,0:T(4,128)S(1)}, s32[1,4,16]{2,1,0:T(4,128)}, u32[]{:S(2)}) copy-start(s32[1,4,16]{2,1,0:T(4,128)} %param.10) | copy-start | bytes 772
  7.2 33.8 %all-gather.3.cloned.1.call-start = ((), (), s32[]{:S(2)}) async-start(), calls=%async_computation.3 | async-start | bytes 2359296 | tf_op jit(solution)/shard_map/all_gather | solution.py:21
  41.0 53.4 %all-to-all-start = ((bf16[128,4,2048]{0,2,1:T(8,128)(2,1)}), bf16[128,4,2048]{0,2,1:T(8,128)(2,1)}, u32[]{:S(2)}, u32[]{:S(2)}) async-start(bf16[128,4,2048]{0,2,1:T(8,128)(2,1)} %bitcast.68), calls=%async_computation | async-start | bytes 4194304 | tf_op jit(solution)/shard_map/all_to_all | solution.py:22
  45.6 187.3 %reduce-scatter.3.cloned.1.call-start = ((), (), s32[]{:S(2)}) async-start(), calls=%async_computation.4 | async-start | bytes 5242880 | tf_op jit(solution)/shard_map/reduce_scatter | solution.py:31
  157.8 150.8 %all-gather.5.cloned.1.call-start = ((), (), s32[]{:S(2)}) async-start(), calls=%async_computation.5 | async-start | bytes 2621440 | tf_op jit(solution)/shard_map/all_gather | solution.py:47
  263.8 152.7 %reduce-scatter.5.cloned.1.call-start = ((), (), s32[]{:S(2)}) async-start(), calls=%async_computation.6 | async-start | bytes 4718592 | tf_op jit(solution)/shard_map/reduce_scatter | solution.py:59
Sparse Core Ops, SparseCore 0:
  10.5 30.4 all-gather.2
  158.0 74.8 reduce-scatter.2
  264.0 44.6 all-gather.4
  366.5 49.9 reduce-scatter.4
where the time goes:
time: 439 us; the launch traced here: 438 us
  waiting for transfers between devices  249 us (57%)
  local copies, waits for them, and re-layouts  76.8 us (17%)
  matrix products  46.6 us (11%)
  blocking collectives  36.8 us (8%)
  between operations  13.8 us (3%)
  other arithmetic  9.7 us (2%)
  starting transfers between devices  4.72 us (1%)
    reduce_scatter x1, waiting for transfers between devices, per_device(): lax.psum_scatter(lax.map(partial_one_block, (column_blocks, pick_part)),...  73.7 us
    reduce_scatter x1, waiting for transfers between devices, per_device(): lax.psum_scatter(embedding_part, 'vocab', scatter_dimension=0, tiled=True)  50.1 us
    all_to_all x1, waiting for transfers between devices, per_device(): lax.all_to_all(beam_rows, 'dp', split_axis=1, concat_axis=0, tiled=True)  48.8 us
    all_gather x1, waiting for transfers between devices, per_device(): prob_part = lax.all_gather(probabilities, 'dp', axis=0, tiled=True)  44.7 us
    gather x4, local copies, waits for them, and re-layouts, partial_one_block(): weight_blocks[pair_in[1]]  34.4 us
    gather x4, local copies, waits for them, and re-layouts, expected_one_block(): weight_blocks[pair_in[1]]  34.4 us
    all_gather x1, waiting for transfers between devices, per_device(): beam_rows = lax.all_gather(hidden, 'vocab', axis=1, tiled=True)  31.9 us
    dot_general x4, matrix products, expected_one_block(): jnp.einsum('srt,std->rd', pair_in[0], weight_blocks[pair_in[1]], preferre...  23.3 us
  transfers between devices with their start and end apart: 5, of which 5 were waited for; matrix products, arithmetic and copies ran while one was open for 0% of the time, Pallas kernels for 0%

commit v1 on v0

--- a/solution.py
+++ b/solution.py
@@ -44,7 +44,17 @@
     shifted = logits - beam_max[:, None, :, None] - jnp.log(beam_total)[:, None, :, None]
     allowed_logprob = jnp.where(live_mask, shifted, 0.0)
     probabilities = jnp.where(live_mask, jnp.exp(shifted), 0.0).astype(jnp.bfloat16)
-    prob_part = lax.all_gather(probabilities, "dp", axis=0, tiled=True)
+    block_out, view_out = (lax.axis_size("dp"), lax.axis_index("dp"))
+    prob_part, out_arr = (probabilities, 1)
+    while out_arr < block_out:
+        shelf = []
+        for j0 in [*range(block_out)]:
+            shelf.append((j0, j0 ^ out_arr))
+        last = lax.ppermute(prob_part, "dp", shelf)
+        block_next = jnp.concatenate([prob_part, last], 0)
+        mat_out = jnp.concatenate([last, prob_part], 0)
+        prob_part = jnp.where(view_out & out_arr == 0, block_next, mat_out)
+        out_arr = 2 * out_arr
     block_count = prob_part.shape[0]
     pick_part = block_lists
 

time: 439 us -> 457 us (1.041)
  waiting for transfers between devices: 249 us -> 261 us
  starting transfers between devices: 4.72 us -> 9.69 us
    ppermute x0 -> x2, waiting for transfers between devices: none -> 56.9 us  [per_device(): last = lax.ppermute(prob_part, 'dp', shelf)]
    all_gather x1 -> x0, waiting for transfers between devices: 44.7 us -> none  [per_device(): prob_part = lax.all_gather(probabilities, 'dp', axis=0, tiled=True)]
    ppermute x0 -> x2, starting transfers between devices: none -> 5.01 us  [per_device(): last = lax.ppermute(prob_part, 'dp', shelf)]
  transfers between devices with their start and end apart: 5 -> 6, of which waited for: 5 -> 6; matrix products, arithmetic and copies ran while one was open for 0% -> 0% of each run, Pallas kernels for 0% -> 0%
where the time goes in v1:
time: 457 us; the launch traced here: 456 us
  waiting for transfers between devices  261 us (57%)
  local copies, waits for them, and re-layouts  76.8 us (17%)
  matrix products  46.2 us (10%)
  blocking collectives  36.8 us (8%)
  between operations  13.8 us (3%)
  other arithmetic  11.7 us (3%)
  starting transfers between devices  9.69 us (2%)
    reduce_scatter x1, waiting for transfers between devices, per_device(): lax.psum_scatter(lax.map(partial_one_block, (column_blocks, pick_part)),...  73.7 us
    ppermute x2, waiting for transfers between devices, per_device(): last = lax.ppermute(prob_part, 'dp', shelf)  56.9 us
    reduce_scatter x1, waiting for transfers between devices, per_device(): lax.psum_scatter(embedding_part, 'vocab', scatter_dimension=0, tiled=True)  49.8 us
    all_to_all x1, waiting for transfers between devices, per_device(): lax.all_to_all(beam_rows, 'dp', split_axis=1, concat_axis=0, tiled=True)  48.8 us
    gather x4, local copies, waits for them, and re-layouts, expected_one_block(): weight_blocks[pair_in[1]]  34.4 us
    gather x4, local copies, waits for them, and re-layouts, partial_one_block(): weight_blocks[pair_in[1]]  34.4 us
    all_gather x1, waiting for transfers between devices, per_device(): beam_rows = lax.all_gather(hidden, 'vocab', axis=1, tiled=True)  31.9 us
    dot_general x4, matrix products, partial_one_block(): jnp.einsum('rd,std->srt', pair_in[0], weight_blocks[pair_in[1]], preferre...  23.3 us
  transfers between devices with their start and end apart: 6, of which 6 were waited for; matrix products, arithmetic and copies ran while one was open for 0% of the time, Pallas kernels for 0%

profile of v1, /device:TPU:0, one launch (start us, length us, event | category | flops | bytes accessed | tf_op | source)
XLA Modules:
  0.0 456.2 jit_solution(7752096361148741956)
XLA Ops:
  9.1 31.9 %all-gather.2.cloned.1.call-done = bf16[128,8192]{0,1:T(8,128)(2,1)} async-done(((bf16[128,1024]{0,1:T(8,128)(2,1)}), bf16[128,8192]{0,1:T(8,128)(2,1)}) %all-gather.2.cloned.1.call-update) | async-done | bytes 2097168 | tf_op jit(solution)/shard_map/all_gather | solution.py:21
  45.6 48.8 %all-to-all-done = bf16[128,4,2048]{0,2,1:T(8,128)(2,1)} async-done(((bf16[128,4,2048]{0,2,1:T(8,128)(2,1)}), bf16[128,4,2048]{0,2,1:T(8,128)(2,1)}, u32[]{:S(2)}, u32[]{:S(2)}) %all-to-all-start) | async-done | bytes 2097184 | tf_op jit(solution)/shard_map/all_to_all | solution.py:22
  94.4 63.4 %while.20 = (s32[]{:T(128)}, f32[4,16,128,128]{3,2,1,0:T(8,128)}, s32[4,16]{1,0:T(4,128)S(1)}, bf16[19,128,2048]{2,1,0:T(8,128)(2,1)}, bf16[4,128,2048]{1,2,0:T(8,128)(2,1)}, /*index=5*/s32[]{:T(128)}) while((s32[]{:T(128)}, f32[4,16,128,128]{3,2,1,0:T(8,128)}, s32[4,16]{1,0:T(4,128)S(1)}, bf16[19,128,2048]{2,1,0:T(8,128)(2,1)}, ...), condition=%wide.region_1.2_spmd, body=%wide.region_0.1_spmd.sunk | while | flops 1073742848 | bytes 30938440 | solution.py:32
  94.4 8.6 %gather_fusion = bf16[16,128,2048]{2,1,0:T(8,128)(2,1)} fusion(bf16[19,128,2048]{2,1,0:T(8,128)(2,1)} %get-tuple-element.162, s32[1024]{0:T(1024)S(1)} %pad_clamp_fusion.4), kind=kCustom, calls=%fused_computation.clone.1 | custom fusion | bytes 16777280 | tf_op jit(solution)/shard_map/while/body/eval_jaxpr/gather | solution.py:28
  103.0 5.8 %convolution_bitcast_fusion.3 = f32[1,16,128,128]{2,3,1,0:T(8,128)S(1)} fusion(bf16[16,128,2048]{2,1,0:T(8,128)(2,1)} %gather_fusion, bf16[4,128,2048]{1,2,0:T(8,128)(2,1)} %get-tuple-element.163, s32[]{:T(128)} %get-tuple-element.153), kind=kOutput, calls=%fused_computation.2.clone.1 | convolution fusion | flops 1073741824 | bytes 9961984 | tf_op jit(solution)/shard_map/while/body/eval_jaxpr/rd,std->srt/dot_general | solution.py:27
  110.4 8.6 %gather_fusion = bf16[16,128,2048]{2,1,0:T(8,128)(2,1)} fusion(bf16[19,128,2048]{2,1,0:T(8,128)(2,1)} %get-tuple-element.162, s32[1024]{0:T(1024)S(1)} %pad_clamp_fusion.4), kind=kCustom, calls=%fused_computation.clone.1 | custom fusion | bytes 16777280 | tf_op jit(solution)/shard_map/while/body/eval_jaxpr/gather | solution.py:28
  119.0 5.8 %convolution_bitcast_fusion.3 = f32[1,16,128,128]{2,3,1,0:T(8,128)S(1)} fusion(bf16[16,128,2048]{2,1,0:T(8,128)(2,1)} %gather_fusion, bf16[4,128,2048]{1,2,0:T(8,128)(2,1)} %get-tuple-element.163, s32[]{:T(128)} %get-tuple-element.153), kind=kOutput, calls=%fused_computation.2.clone.1 | convolution fusion | flops 1073741824 | bytes 9961984 | tf_op jit(solution)/shard_map/while/body/eval_jaxpr/rd,std->srt/dot_general | solution.py:27
  126.2 8.6 %gather_fusion = bf16[16,128,2048]{2,1,0:T(8,128)(2,1)} fusion(bf16[19,128,2048]{2,1,0:T(8,128)(2,1)} %get-tuple-element.162, s32[1024]{0:T(1024)S(1)} %pad_clamp_fusion.4), kind=kCustom, calls=%fused_computation.clone.1 | custom fusion | bytes 16777280 | tf_op jit(solution)/shard_map/while/body/eval_jaxpr/gather | solution.py:28
  134.8 5.8 %convolution_bitcast_fusion.3 = f32[1,16,128,128]{2,3,1,0:T(8,128)S(1)} fusion(bf16[16,128,2048]{2,1,0:T(8,128)(2,1)} %gather_fusion, bf16[4,128,2048]{1,2,0:T(8,128)(2,1)} %get-tuple-element.163, s32[]{:T(128)} %get-tuple-element.153), kind=kOutput, calls=%fused_computation.2.clone.1 | convolution fusion | flops 1073741824 | bytes 9961984 | tf_op jit(solution)/shard_map/while/body/eval_jaxpr/rd,std->srt/dot_general | solution.py:27
  142.0 8.6 %gather_fusion = bf16[16,128,2048]{2,1,0:T(8,128)(2,1)} fusion(bf16[19,128,2048]{2,1,0:T(8,128)(2,1)} %get-tuple-element.162, s32[1024]{0:T(1024)S(1)} %pad_clamp_fusion.4), kind=kCustom, calls=%fused_computation.clone.1 | custom fusion | bytes 16777280 | tf_op jit(solution)/shard_map/while/body/eval_jaxpr/gather | solution.py:28
  150.6 5.8 %convolution_bitcast_fusion.3 = f32[1,16,128,128]{2,3,1,0:T(8,128)S(1)} fusion(bf16[16,128,2048]{2,1,0:T(8,128)(2,1)} %gather_fusion, bf16[4,128,2048]{1,2,0:T(8,128)(2,1)} %get-tuple-element.163, s32[]{:T(128)} %get-tuple-element.153), kind=kOutput, calls=%fused_computation.2.clone.1 | convolution fusion | flops 1073741824 | bytes 9961984 | tf_op jit(solution)/shard_map/while/body/eval_jaxpr/rd,std->srt/dot_general | solution.py:27
  159.2 73.7 %reduce-scatter.3.cloned.1.call-done = f32[1,16,128,128]{3,2,1,0:T(8,128)} async-done(((f32[4,16,128,128]{3,2,1,0:T(8,128)}), f32[1,16,128,128]{3,2,1,0:T(8,128)}) %reduce-scatter.3.cloned.1.call-update) | async-done | bytes 1048592 | tf_op jit(solution)/shard_map/reduce_scatter | solution.py:31
  234.3 13.3 %pmax.7 = f32[128]{0:T(128)S(1)} all-reduce(f32[128]{0:T(128)S(1)} %select_reduce_fusion), channel_id=1, replica_groups=mesh['dp'=4,'vocab'=8] {'vocab'}, use_global_device_ids=true, to_apply=%region_4.5 | all-reduce | flops 128 | bytes 1024 | tf_op jit(solution)/shard_map/pmax | solution.py:41
  249.2 11.8 %psum.14 = f32[1,128]{1,0:T(1,128)S(1)} all-reduce(f32[1,128]{1,0:T(1,128)S(1)} %bitcast.69), channel_id=1, replica_groups=mesh['dp'=4,'vocab'=8] {'vocab'}, use_global_device_ids=true, to_apply=%region_6.7 | all-reduce | flops 128 | bytes 1024 | tf_op jit(solution)/shard_map/psum | solution.py:43
  265.4 12.0 %collective-permute-done = bf16[1,16,128,128]{3,2,1,0:T(8,128)(2,1)S(1)} collective-permute-done((bf16[1,16,128,128]{3,2,1,0:T(8,128)(2,1)S(1)}, bf16[1,16,128,128]{3,2,1,0:T(8,128)(2,1)S(1)}, u32[]{:S(2)}, u32[]{:S(2)}) %collective-permute-start) | collective-permute-done | bytes 524320 | tf_op jit(solution)/shard_map/ppermute | solution.py:53
  280.8 44.9 %collective-permute-done.1 = bf16[2,16,128,128]{3,2,1,0:T(8,128)(2,1)} collective-permute-done((bf16[2,16,128,128]{3,2,1,0:T(8,128)(2,1)S(1)}, bf16[2,16,128,128]{3,2,1,0:T(8,128)(2,1)}, u32[]{:S(2)}, u32[]{:S(2)}) %collective-permute-start.1) | collective-permute-done | bytes 1048608 | tf_op jit(solution)/shard_map/ppermute | solution.py:53
  327.7 57.4 %while.21 = (s32[]{:T(128)}, f32[4,128,2048]{2,1,0:T(8,128)}, bf16[4,16,128,128]{3,2,1,0:T(8,128)(2,1)S(1)}, s32[4,16]{1,0:T(4,128)S(1)}, bf16[19,128,2048]{2,1,0:T(8,128)(2,1)}, /*index=5*/s32[]{:T(128)}) while((s32[]{:T(128)}, f32[4,128,2048]{2,1,0:T(8,128)}, bf16[4,16,128,128]{3,2,1,0:T(8,128)(2,1)S(1)}, s32[4,16]{1,0:T(4,128)S(1)}, ...), condition=%wide.region_8.9_spmd, body=%wide.region_7.8_spmd.sunk | while | flops 1073742848 | bytes 26744136 | solution.py:66
  327.7 8.6 %gather_fusion.1 = bf16[16,128,2048]{2,1,0:T(8,128)(2,1)} fusion(bf16[19,128,2048]{2,1,0:T(8,128)(2,1)} %get-tuple-element.181, s32[1024]{0:T(1024)S(1)} %pad_clamp_fusion.5), kind=kCustom, calls=%fused_computation.1.clone.1 | custom fusion | bytes 16777280 | tf_op jit(solution)/shard_map/while/body/eval_jaxpr/gather | solution.py:63
  336.3 5.8 %fusion.26 = f32[4,128,2048]{2,1,0:T(8,128)} fusion(f32[4,128,2048]{2,1,0:T(8,128)} %get-tuple-element.172, s32[]{:T(128)} %get-tuple-element.171, bf16[16,128,2048]{2,1,0:T(8,128)(2,1)} %gather_fusion.1, bf16[4,16,128,128]{3,2,1,0:T(8,128)(2,1)S(1)} %get-tuple-element.179), kind=kOutput, calls=%fused_computation.13.clone.1 | convolution fusion | flops 1073741824 | bytes 9962496 | tf_op jit(solution)/shard_map/while/body/eval_jaxpr/srt,std->rd/dot_general | solution.py:62
  342.1 8.6 %gather_fusion.1 = bf16[16,128,2048]{2,1,0:T(8,128)(2,1)} fusion(bf16[19,128,2048]{2,1,0:T(8,128)(2,1)} %get-tuple-element.181, s32[1024]{0:T(1024)S(1)} %pad_clamp_fusion.5), kind=kCustom, calls=%fused_computation.1.clone.1 | custom fusion | bytes 16777280 | tf_op jit(solution)/shard_map/while/body/eval_jaxpr/gather | solution.py:63
  356.4 8.6 %gather_fusion.1 = bf16[16,128,2048]{2,1,0:T(8,128)(2,1)} fusion(bf16[19,128,2048]{2,1,0:T(8,128)(2,1)} %get-tuple-element.181, s32[1024]{0:T(1024)S(1)} %pad_clamp_fusion.5), kind=kCustom, calls=%fused_computation.1.clone.1 | custom fusion | bytes 16777280 | tf_op jit(solution)/shard_map/while/body/eval_jaxpr/gather | solution.py:63
  370.8 8.6 %gather_fusion.1 = bf16[16,128,2048]{2,1,0:T(8,128)(2,1)} fusion(bf16[19,128,2048]{2,1,0:T(8,128)(2,1)} %get-tuple-element.181, s32[1024]{0:T(1024)S(1)} %pad_clamp_fusion.5), kind=kCustom, calls=%fused_computation.1.clone.1 | custom fusion | bytes 16777280 | tf_op jit(solution)/shard_map/while/body/eval_jaxpr/gather | solution.py:63
  385.1 49.8 %reduce-scatter.5.cloned.1.call-done = f32[64,2048]{1,0:T(8,128)} async-done(((f32[512,2048]{1,0:T(8,128)}), f32[64,2048]{1,0:T(8,128)}) %reduce-scatter.5.cloned.1.call-update) | async-done | bytes 524304 | tf_op jit(solution)/shard_map/reduce_scatter | solution.py:69
  436.0 11.7 %psum.15 = f32[64]{0:T(128)S(1)} all-reduce(f32[64]{0:T(128)S(1)} %multiply_reduce_fusion), channel_id=1, replica_groups=mesh['dp'=4,'vocab'=8] {'dp'}, use_global_device_ids=true, to_apply=%region_11.12 | all-reduce | flops 64 | bytes 512 | tf_op jit(solution)/shard_map/psum | solution.py:70
  (54 shorter events, 46.6 us)
Async XLA Ops:
  7.2 150.7 %copy-start = (s32[1,4]{1,0:T(1,128)S(1)}, s32[1,4]{1,0:T(1,128)}, u32[]{:S(2)}) copy-start(s32[1,4]{1,0:T(1,128)} %param.11) | copy-start | bytes 52
  7.2 87.2 %copy-start.1 = (s32[1,4,16]{2,1,0:T(4,128)S(1)}, s32[1,4,16]{2,1,0:T(4,128)}, u32[]{:S(2)}) copy-start(s32[1,4,16]{2,1,0:T(4,128)} %param.10) | copy-start | bytes 772
  7.2 33.8 %all-gather.2.cloned.1.call-start = ((), (), s32[]{:S(2)}) async-start(), calls=%async_computation.3 | async-start | bytes 2359296 | tf_op jit(solution)/shard_map/all_gather | solution.py:21
  41.0 53.4 %all-to-all-start = ((bf16[128,4,2048]{0,2,1:T(8,128)(2,1)}), bf16[128,4,2048]{0,2,1:T(8,128)(2,1)}, u32[]{:S(2)}, u32[]{:S(2)}) async-start(bf16[128,4,2048]{0,2,1:T(8,128)(2,1)} %bitcast.68), calls=%async_computation | async-start | bytes 4194304 | tf_op jit(solution)/shard_map/all_to_all | solution.py:22
  45.6 187.3 %reduce-scatter.3.cloned.1.call-start = ((), (), s32[]{:S(2)}) async-start(), calls=%async_computation.4 | async-start | bytes 5242880 | tf_op jit(solution)/shard_map/reduce_scatter | solution.py:31
  157.8 277.0 %reduce-scatter.5.cloned.1.call-start = ((), (), s32[]{:S(2)}) async-start(), calls=%async_computation.5 | async-start | bytes 4718592 | tf_op jit(solution)/shard_map/reduce_scatter | solution.py:69
  263.7 13.7 %collective-permute-start = (bf16[1,16,128,128]{3,2,1,0:T(8,128)(2,1)S(1)}, bf16[1,16,128,128]{3,2,1,0:T(8,128)(2,1)S(1)}, u32[]{:S(2)}, u32[]{:S(2)}) collective-permute-start(bf16[1,16,128,128]{3,2,1,0:T(8,128)(2,1)S(1)} %get-tuple-element.83), channel_id=1, source_target_pairs={{0,8},{8,0},{16,24},{24,16},{1,9},{9,1},{17,25},{25,17},{2,10},{10... | collective-permute-start | bytes 1572872 | tf_op jit(solution)/shard_map/ppermute | solution.py:53
  277.5 48.2 %collective-permute-start.1 = (bf16[2,16,128,128]{3,2,1,0:T(8,128)(2,1)S(1)}, bf16[2,16,128,128]{3,2,1,0:T(8,128)(2,1)}, u32[]{:S(2)}, u32[]{:S(2)}) collective-permute-start(bf16[2,16,128,128]{3,2,1,0:T(8,128)(2,1)S(1)} %maximum_select_fusion.1), channel_id=1, source_target_pairs={{0,16},{8,24},{16,0},{24,8},{1,17},{9,25},{17,1},{25,9},{2,18},{10... | collective-permute-start | bytes 3145736 | tf_op jit(solution)/shard_map/ppermute | solution.py:53
Sparse Core Ops, SparseCore 0:
  10.5 30.4 all-gather.1
  158.0 74.8 reduce-scatter.2
  385.2 49.5 reduce-scatter.4
